TPU v7x, 256 devices: a whole 4x4x8 slice. The times are simulated.
256 devices in a mesh: seq: 64 (over z, y, core), mp: 4 (over x).
Axes of the slice: x: 4, y: 4, z: 8, core: 2. Of those that a mesh axis runs over, the one named last changes fastest.
Arguments:
- patches: bfloat16 [262144, 1280], P('seq'), may hold values from -2 to 2
- w_qkv: bfloat16 [1280, 3840], P('seq', 'mp'), as said below
- w_out: bfloat16 [1280, 1280], P('mp', 'seq'), may hold values from -0.15625 to 0.15625
- page_rows: int32 [64], replicated, may hold values from 32 to 64, as said below
- page_cols: int32 [64], replicated, may hold values from 32 to 64, as said below
- window_slot: int32 [64, 64], replicated, may hold values from 0 to 63, each once within a row
Outputs:
- blocks: bfloat16 [262144, 1280], P('seq', 'mp')
Inputs may be any that keep to these rules, and one draw needn't show every extreme that they name: `page_rows`: page heights, multiples of 16; some page has the largest. `page_cols`: page widths, multiples of 16; some page has the largest. `window_slot`: each row is a permutation. `w_qkv`: entries of order at most 5.5 / sqrt(1280).
All inputs are finite; a program needn't handle non-finite values.
Results may differ from a plain program's by a relative error of at most 0.012.
Values may be sent and summed in bfloat16 or wider, within the bound.
No kernel may reach another device: no remote copies, remote signals or barrier semaphores. Data moves between devices by JAX's collectives and lax.ppermute only.
A program may use at most 192 MiB of HBM per device.

v0:
```python
import jax
import jax.numpy as jnp
from jax import lax
from jax.sharding import PartitionSpec as P

HD = 80
WS = 8
QUARTERS = 4
EPSILON = 1e-06


def angle_tables(row_place, column_place, head_size):
    quarter = head_size // 4
    frequency = 1.0 / 10000.0 ** (jnp.arange(quarter, dtype=jnp.float32) * 2.0 / (head_size // 2))
    angles = jnp.concatenate(
        [
            row_place[..., None].astype(jnp.float32) * frequency,
            column_place[..., None].astype(jnp.float32) * frequency,
        ],
        axis=-1,
    )
    angles = jnp.concatenate([angles, angles], axis=-1)
    return (jnp.cos(angles), jnp.sin(angles))


def slot_positions(page_widths, slot_table, slot_numbers, window_side):
    matches = slot_table[:, :, None] == slot_numbers[None, None, :]
    ordinal = jnp.arange(slot_table.shape[1], dtype=jnp.int32)
    window = jnp.sum(jnp.where(matches, ordinal[None, :, None], 0), axis=1)
    across = page_widths // window_side
    window_row = window // across[:, None]
    window_column = window % across[:, None]
    unit_side = window_side // 2
    position = jnp.arange(window_side * window_side, dtype=jnp.int32)
    merge_unit = position // 4
    corner = position % 4
    inner_row = merge_unit // unit_side * 2 + corner // 2
    inner_column = merge_unit % unit_side * 2 + corner % 2
    row_place = window_row[:, :, None] * window_side + inner_row
    column_place = window_column[:, :, None] * window_side + inner_column
    return (row_place, column_place)


def block_sources(height, page_width, slot_row, block_count):
    across = page_width // WS
    block = jnp.arange(block_count, dtype=jnp.int32)
    band = block // across
    column = block % across
    window_row = band // QUARTERS
    quarter = band % QUARTERS
    live = window_row < height // WS
    window = jnp.where(live, window_row * across + column, 0)
    ordinal = jnp.arange(slot_row.shape[0], dtype=jnp.int32)
    slot = jnp.sum(jnp.where(window[:, None] == ordinal[None, :], slot_row[None, :], 0), axis=1)
    return (slot * QUARTERS + quarter, live)


def normalize(block_in):
    values = block_in.astype(jnp.float32)
    factor = lax.rsqrt(jnp.mean(values * values, axis=-1, keepdims=True) + EPSILON)
    return (values * factor).astype(jnp.bfloat16)


def rotated_columns(weight):
    half = weight.shape[-1] // 2
    return jnp.concatenate([-weight[..., half:], weight[..., :half]], axis=-1)


def local(patches, w_qkv, w_out, page_rows, page_cols, window_slot):
    seq_index = lax.axis_index("seq")
    seq_count = lax.axis_size("seq")
    mp_index = lax.axis_index("mp")
    page_count = window_slot.shape[0]
    slot_count = window_slot.shape[1]
    slots_held = slot_count // seq_count
    window_tokens = WS * WS
    quarter_tokens = window_tokens // QUARTERS
    model_width = patches.shape[1]
    windows = patches.shape[0] // window_tokens
    own_rows = w_qkv.shape[0]
    heads = w_qkv.shape[1] // (3 * HD)
    qkv = w_qkv.reshape(own_rows, heads, 3, HD)
    w_q = qkv[:, :, 0]
    w_k = qkv[:, :, 1]
    fused_rows = jnp.concatenate(
        [
            w_q.reshape(own_rows, heads * HD),
            w_k.reshape(own_rows, heads * HD),
            rotated_columns(w_q).reshape(own_rows, heads * HD),
            rotated_columns(w_k).reshape(own_rows, heads * HD),
            qkv[:, :, 2].reshape(own_rows, heads * HD),
            w_out.T,
        ],
        axis=1,
    )
    joined = lax.all_gather(fused_rows, "seq", axis=0, tiled=True)
    fused = joined[:, : 5 * heads * HD]
    out_rows_t = joined[:, 5 * heads * HD :]
    out_full_t = lax.all_gather(out_rows_t, "mp", axis=1, tiled=True)
    slot_numbers = seq_index * slots_held + jnp.arange(slots_held, dtype=jnp.int32)
    row_place, column_place = slot_positions(page_cols, window_slot, slot_numbers, WS)
    cosine, sine = angle_tables(
        row_place.reshape(-1, window_tokens), column_place.reshape(-1, window_tokens), HD
    )
    cosine = jnp.tile(cosine.reshape(-1, HD), (1, 2 * heads))
    sine = jnp.tile(sine.reshape(-1, HD), (1, 2 * heads))
    normed = normalize(patches)
    projected = jnp.dot(normed, fused, preferred_element_type=jnp.float32)
    width = heads * HD
    turned = projected[:, : 2 * width] * cosine + projected[:, 2 * width : 4 * width] * sine
    turned = turned.astype(jnp.bfloat16).reshape(windows, window_tokens, 2 * width)
    queries = turned[:, :, :width]
    key_block = turned[:, :, width:]
    values = projected[:, 4 * width :].astype(jnp.bfloat16).reshape(windows, window_tokens, width)
    lane_head = jnp.arange(width, dtype=jnp.int32) // HD
    scale = 1.0 / HD**0.5
    mixed = jnp.zeros((windows, window_tokens, width), jnp.float32)
    for head in range(heads):
        mask = lane_head == head
        picked = jnp.where(mask, queries, jnp.zeros_like(queries))
        scores = (
            jnp.einsum("wqd,wkd->wqk", picked, key_block, preferred_element_type=jnp.float32)
            * scale
        )
        row_max = jnp.max(scores, axis=-1, keepdims=True)
        lifted = jnp.exp(scores - row_max)
        weights = (lifted / jnp.sum(lifted, axis=-1, keepdims=True)).astype(jnp.bfloat16)
        own_values = jnp.where(mask, values, jnp.zeros_like(values))
        mixed = mixed + jnp.einsum(
            "wqk,wkd->wqd", weights, own_values, preferred_element_type=jnp.float32
        )
    mixed = mixed.astype(jnp.bfloat16)
    spread = mixed.reshape(windows, QUARTERS, quarter_tokens, width)
    gathered = lax.all_to_all(spread, "mp", split_axis=1, concat_axis=1, tiled=True)
    out_grouped = out_full_t.reshape(model_width, QUARTERS, width)
    branch = lax.dot_general(
        gathered, out_grouped, (((1, 3), (1, 2)), ((), ())), preferred_element_type=jnp.float32
    )
    branch = branch.reshape(windows * quarter_tokens, model_width)
    residual = patches.reshape(windows, QUARTERS, quarter_tokens, model_width)
    residual = lax.dynamic_index_in_dim(residual, mp_index, 1, keepdims=False)
    residual = residual.reshape(windows * quarter_tokens, model_width).astype(jnp.float32)
    block_out = (residual + branch).astype(jnp.bfloat16)
    share_width = model_width // QUARTERS
    sectioned = block_out.reshape(page_count, quarter_tokens, QUARTERS, share_width)
    sectioned = jnp.transpose(sectioned, (0, 2, 1, 3)).reshape(
        page_count * QUARTERS, quarter_tokens, share_width
    )
    landed = lax.all_to_all(sectioned, ("seq", "mp"), split_axis=0, concat_axis=0, tiled=True)
    own_pages = page_count // seq_count
    first_page = seq_index * own_pages
    heights = lax.dynamic_slice_in_dim(page_rows, first_page, own_pages, 0)
    widths = lax.dynamic_slice_in_dim(page_cols, first_page, own_pages, 0)
    slot_rows = lax.dynamic_slice_in_dim(window_slot, first_page, own_pages, 0)
    block_count = slot_count * QUARTERS // own_pages
    landed = landed.reshape(own_pages, block_count, quarter_tokens, share_width)

    def regroup(received, height, page_width, slot_row):
        source, live = block_sources(height, page_width, slot_row, block_count)
        picked = jnp.take(received, source, axis=0)
        return jnp.where(live[:, None, None], picked, jnp.zeros_like(picked))

    merged = jax.vmap(regroup)(landed, heights, widths, slot_rows)
    return merged.reshape(-1, share_width)


def solution(mesh):
    return jax.shard_map(
        local,
        mesh=mesh,
        in_specs=(P("seq", None), P("seq", "mp"), P("mp", "seq"), P(), P(), P()),
        out_specs=P("seq", "mp"),
        check_vma=False,
    )
```

profile of v0, /device:TPU:1, one launch (start us, length us, event | category | flops | bytes accessed | tf_op | source)
XLA Modules:
  0.0 355.9 jit_solution(10992189034661572990)
XLA Ops:
  8.7 1.5 concatenate.24
  12.5 6.1 %fusion.4 = f32[4096]{0:T(1024)S(1)} fusion(bf16[4096,1280]{1,0:T(8,128)(2,1)} %param.6), kind=kLoop, calls=%fused_computation.7 | loop fusion | flops 15724544 | bytes 10502144 | tf_op jit(solution)/shard_map/reduce_sum | solution.py:60
  18.7 4.8 %fusion.69 = (f32[4096,80]{0,1:T(8,128)S(1)}, f32[4096,80]{0,1:T(8,128)S(1)}) fusion(f32[4096,20]{0,1:T(8,128)S(1)} %get-tuple-element.19, f32[4096,20]{0,1:T(8,128)S(1)} %get-tuple-element.18), kind=kLoop, calls=%fused_computation.88 | loop fusion | flops 983040 | bytes 3276800 | tf_op jit(solution)/shard_map/cos | solution.py:23
  23.5 71.3 %all-gather.6.cloned.1.call-done = bf16[64,20,1920]{2,1,0:T(8,128)(2,1)} async-done(((bf16[1,20,1920]{2,1,0:T(8,128)(2,1)}), bf16[64,20,1920]{2,1,0:T(8,128)(2,1)}) %all-gather.6.cloned.1.call-update) | async-done | bytes 4915216 | tf_op jit(solution)/shard_map/all_gather | solution.py:96
  94.8 7.5 %reshape.662 = bf16[1280,1920]{1,0:T(8,128)(2,1)} reshape(bf16[64,20,1920]{2,1,0:T(8,128)(2,1)} %all-gather.6.cloned.1.call-done) | data formatting | bytes 9830400
  102.3 2.6 slice.72
  104.9 2.2 copy.67
  107.2 23.8 %fusion.6 = f32[4096,1600]{0,1:T(8,128)} fusion(bf16[4096,1280]{1,0:T(8,128)(2,1)} %param.6, f32[4096]{0:T(1024)S(1)} %add_rsqrt_fusion, bf16[1280,1920]{1,0:T(8,128)(2,1)} %reshape.662), kind=kOutput, calls=%fused_computation.9 | convolution fusion | flops 16792944640 | bytes 40976384 | tf_op jit(solution)/shard_map/dot_general | solution.py:108
  131.0 4.4 %slice.125 = bf16[4096,320]{0,1:T(8,128)(2,1)} slice(f32[4096,1600]{0,1:T(8,128)} %fusion.6), slice={[0:4096], [1280:1600]} | slice | bytes 5242880 | tf_op jit(solution)/shard_map/slice | solution.py:114
  135.4 10.4 %fusion.9 = bf16[4096,640]{0,1:T(8,128)(2,1)} fusion(f32[4096,1600]{0,1:T(8,128)} %fusion.6, f32[4096,80]{0,1:T(8,128)S(1)} %get-tuple-element.11, f32[4096,80]{0,1:T(8,128)S(1)} %get-tuple-element.10), kind=kLoop, calls=%fused_computation.12 | loop fusion | flops 10485760 | bytes 28835840 | tf_op jit(solution)/shard_map/convert_element_type | solution.py:111
  145.8 7.9 %copy.60 = bf16[4096,640]{1,0:T(8,128)(2,1)} copy(bf16[4096,640]{0,1:T(8,128)(2,1)} %fusion.9) | data formatting | bytes 10485760 | tf_op jit(solution)/shard_map/convert_element_type | solution.py:111
  153.7 3.5 copy.61
  157.2 5.4 %fusion.20 = f32[64,64,64]{1,2,0:T(8,128)S(1)} fusion(pred[320]{0:T(512)(128)(4,1)S(1)} %broadcast_compare_fusion.1, bf16[64,64,640]{2,1,0:T(8,128)(2,1)} %bitcast.54), kind=kOutput, calls=%fused_computation.28 | convolution fusion | flops 169082880 | bytes 7340352 | tf_op jit(solution)/shard_map/wqd,wkd->wqk/dot_general | solution.py:122
  164.0 1.4 fusion.16
  165.4 1.4 fusion.28
  166.7 1.4 fusion.24
  170.1 5.4 %fusion.22 = f32[64,64,320]{2,1,0:T(8,128)} fusion(bf16[64,64,320]{2,1,0:T(8,128)(2,1)S(1)} %bitcast.50, pred[320]{0:T(512)(128)(4,1)S(1)} %broadcast_compare_fusion.3, f32[64,64]{1,0:T(8,128)S(1)} %fusion.127, f32[64,64,64]{1,2,0:T(8,128)} %copy-done.7), kind=kOutput, calls=%fused_computation.30 | convolution fusion | flops 170135616 | bytes 8929600 | tf_op jit(solution)/shard_map/wqk,wkd->wqd/dot_general | solution.py:129
  175.5 5.4 %fusion.14 = f32[64,64,320]{2,1,0:T(8,128)} fusion(bf16[64,64,320]{2,1,0:T(8,128)(2,1)S(1)} %bitcast.51, pred[320]{0:T(512)(128)(4,1)S(1)} %broadcast_compare_fusion, f32[64,64]{1,0:T(8,128)S(1)} %fusion.125, f32[64,64,64]{1,2,0:T(8,128)} %copy-done.6), kind=kOutput, calls=%fused_computation.22 | convolution fusion | flops 170135616 | bytes 8929600 | tf_op jit(solution)/shard_map/wqk,wkd->wqd/dot_general | solution.py:129
  180.9 5.3 %fusion.18 = f32[64,64,320]{2,1,0:T(8,128)} fusion(bf16[64,64,320]{2,1,0:T(8,128)(2,1)S(1)} %bitcast.52, pred[320]{0:T(512)(128)(4,1)S(1)} %broadcast_compare_fusion.1, f32[64,64]{1,0:T(8,128)S(1)} %fusion.126, f32[64,64,64]{1,2,0:T(8,128)} %copy-done.5), kind=kOutput, calls=%fused_computation.26 | convolution fusion | flops 170135616 | bytes 8929600 | tf_op jit(solution)/shard_map/wqk,wkd->wqd/dot_general | solution.py:129
  186.2 9.9 %add_convert_fusion = bf16[64,64,320]{2,1,0:T(8,128)(2,1)S(1)} fusion(f32[64,64,320]{2,1,0:T(8,128)} %fusion.14, f32[64,64,320]{2,1,0:T(8,128)} %fusion.18, f32[64,64,320]{2,1,0:T(8,128)} %fusion.22, bf16[64,64,320]{2,1,0:T(8,128)(2,1)} %bitcast.53, pred[320]{0:T(512)(128)(4,1)S(1)} %broadcast_compare_fusion.2, f32[64,64]{1,0:T(8,128)S(1)} %fusion.128, ...), kind=kOutput, calls=%fused_computation.15 | convolution fusion | flops 175378496 | bytes 22036800 | tf_op jit(solution)/shard_map/wqk,wkd->wqd/dot_general | solution.py:129
  196.1 2.0 copy.66
  198.1 3.9 %all-to-all-start = ((bf16[64,4,16,320]{3,2,0,1:T(8,128)(2,1)}), bf16[64,4,16,320]{3,2,0,1:T(8,128)(2,1)S(1)}, u32[]{:S(2)}, u32[]{:S(2)}) async-start(bf16[64,4,16,320]{3,2,0,1:T(8,128)(2,1)} %copy.66), calls=%async_computation | async-start | bytes 6291456 | tf_op jit(solution)/shard_map/all_to_all | solution.py:134
  201.9 3.4 constant_dynamic-slice_fusion
  205.4 33.7 %all-to-all-done = bf16[64,4,16,320]{3,2,0,1:T(8,128)(2,1)S(1)} async-done(((bf16[64,4,16,320]{3,2,0,1:T(8,128)(2,1)}), bf16[64,4,16,320]{3,2,0,1:T(8,128)(2,1)S(1)}, u32[]{:S(2)}, u32[]{:S(2)}) %all-to-all-start) | async-done | bytes 2621472 | tf_op jit(solution)/shard_map/all_to_all | solution.py:134
  239.0 7.3 %fusion.11 = bf16[1024,1280]{1,0:T(8,128)(2,1)} fusion(bf16[1024,1280]{1,0:T(8,128)(2,1)} %bitcast.59, bf16[1024,4,320]{2,0,1:T(8,128)(2,1)S(1)} %bitcast.58, bf16[1280,4,320]{0,2,1:T(8,128)(2,1)} %bitcast.63), kind=kOutput, calls=%fused_computation.18 | convolution fusion | flops 3359375360 | bytes 11141120 | tf_op jit(solution)/shard_map/dot_general | solution.py:136
  246.3 6.1 %reshape.648 = bf16[64,16,4,320]{3,2,1,0:T(4,128)(2,1)S(1)} reshape(bf16[1024,1280]{1,0:T(8,128)(2,1)} %fusion.11) | data formatting | bytes 5242880 | tf_op jit(solution)/shard_map/reshape | solution.py:145
  252.4 2.4 copy.69
  254.8 7.8 %all-to-all-start.1 = ((bf16[256,16,320]{2,1,0:T(8,128)(2,1)}), bf16[256,16,320]{2,1,0:T(8,128)(2,1)S(1)}, u32[]{:S(2)}, u32[]{:S(2)}) async-start(bf16[256,16,320]{2,1,0:T(8,128)(2,1)} %bitcast.48), calls=%async_computation.1 | async-start | bytes 6291456 | tf_op jit(solution)/shard_map/all_to_all | solution.py:149
  270.6 67.9 %all-to-all-done.1 = bf16[256,16,320]{2,1,0:T(8,128)(2,1)S(1)} async-done(((bf16[256,16,320]{2,1,0:T(8,128)(2,1)}), bf16[256,16,320]{2,1,0:T(8,128)(2,1)S(1)}, u32[]{:S(2)}, u32[]{:S(2)}) %all-to-all-start.1) | async-done | bytes 2621472 | tf_op jit(solution)/shard_map/all_to_all | solution.py:149
  338.6 2.7 gather_fusion
  341.3 5.0 %fusion.13 = bf16[4096,320]{1,0:T(8,128)(2,1)S(1)} fusion(bf16[256,16,320]{2,1,0:T(8,128)(2,1)} %gather_fusion, pred[4096]{0:T(1024)(128)(4,1)S(1)} %broadcast_in_dim.141, pred[4096]{0:T(1024)(128)(4,1)S(1)} %broadcast_in_dim.135), kind=kLoop, calls=%fused_computation.21 | loop fusion | flops 2621440 | bytes 5251072 | tf_op jit(solution)/shard_map/vmap(jit(_where))/select_n | solution.py:161
  346.3 2.7 copy.70
  (66 shorter events, 10.7 us)
Async XLA Ops:
  6.5 88.3 %all-gather.6.cloned.1.call-start = ((), (), s32[]{:S(2)}) async-start(), calls=%async_computation.3 | async-start | bytes 5990400 | tf_op jit(solution)/shard_map/all_gather | solution.py:96
  10.2 228.8 %all-gather.4.cloned.1.call-start = ((), (), s32[]{:S(2)}) async-start(), calls=%async_computation.2 | async-start | bytes 4096000 | tf_op jit(solution)/shard_map/all_gather | solution.py:99
  157.2 23.6 %copy-start = (bf16[4096,320]{1,0:T(8,128)(2,1)}, bf16[4096,320]{1,0:T(8,128)(2,1)S(1)}, u32[]{:S(2)}) copy-start(bf16[4096,320]{1,0:T(8,128)(2,1)S(1)} %copy.61) | copy-start | bytes 7864324
  157.2 6.7 %copy-start.1 = (bf16[4096,640]{1,0:T(8,128)(2,1)S(1)}, bf16[4096,640]{1,0:T(8,128)(2,1)}, u32[]{:S(2)}) copy-start(bf16[4096,640]{1,0:T(8,128)(2,1)} %copy.60) | copy-start | bytes 15728644
  162.6 1.4 copy-start.5
  165.3 2.8 copy-start.6
  166.7 2.7 copy-start.2
  168.1 2.0 copy-start.7
  198.1 41.0 %all-to-all-start = ((bf16[64,4,16,320]{3,2,0,1:T(8,128)(2,1)}), bf16[64,4,16,320]{3,2,0,1:T(8,128)(2,1)S(1)}, u32[]{:S(2)}, u32[]{:S(2)}) async-start(bf16[64,4,16,320]{3,2,0,1:T(8,128)(2,1)} %copy.66), calls=%async_computation | async-start | bytes 6291456 | tf_op jit(solution)/shard_map/all_to_all | solution.py:134
  254.8 7.8 %copy-start.3 = (s32[64]{0:T(128)S(1)}, s32[64]{0:T(128)}, u32[]{:S(2)}) copy-start(s32[64]{0:T(128)} %param.10) | copy-start | bytes 772
  254.8 11.0 %copy-start.4 = (s32[64]{0:T(128)S(1)}, s32[64]{0:T(128)}, u32[]{:S(2)}) copy-start(s32[64]{0:T(128)} %param.9) | copy-start | bytes 772
  254.8 83.8 %all-to-all-start.1 = ((bf16[256,16,320]{2,1,0:T(8,128)(2,1)}), bf16[256,16,320]{2,1,0:T(8,128)(2,1)S(1)}, u32[]{:S(2)}, u32[]{:S(2)}) async-start(bf16[256,16,320]{2,1,0:T(8,128)(2,1)} %bitcast.48), calls=%async_computation.1 | async-start | bytes 6291456 | tf_op jit(solution)/shard_map/all_to_all | solution.py:149
Sparse Core Ops, SparseCore 0:
  10.4 84.3 all-gather.5
  107.3 39.4 all-gather.3
where the time goes:
time: 357 us; the launch traced here: 356 us
  waiting for transfers between devices  173 us (48%)
  matrix products  66.5 us (19%)
  local copies, waits for them, and re-layouts  54 us (15%)
  other arithmetic  31.8 us (9%)
  between operations  18.9 us (5%)
  starting transfers between devices  11.7 us (3%)
    all_gather x1, waiting for transfers between devices, local(): joined = lax.all_gather(fused_rows, 'seq', axis=0, tiled=True)  71.3 us
    all_to_all x1, waiting for transfers between devices, local(): lax.all_to_all(sectioned, ('seq', 'mp'), split_axis=0, concat_axis=0, til...  67.9 us
    all_to_all x1, waiting for transfers between devices, local(): lax.all_to_all(spread, 'mp', split_axis=1, concat_axis=1, tiled=True)  33.7 us
    dot_general x4, matrix products, local(): jnp.einsum('wqk,wkd->wqd', weights, own_values, preferred_element_type=jn...  26 us
    dot_general x1, matrix products, local(): projected = jnp.dot(normed, fused, preferred_element_type=jnp.float32)  23.8 us
    convert_element_type x1, other arithmetic, local(): turned.astype(jnp.bfloat16).reshape(windows, window_tokens, 2 * width)  10.4 us
    dot_general x4, matrix products, local(): jnp.einsum('wqd,wkd->wqk', picked, key_block, preferred_element_type=jnp....  9.45 us
    reshape x2, local copies, waits for them, and re-layouts, local(): block_out.reshape(page_count, quarter_tokens, QUARTERS, share_width)  8.5 us
  transfers between devices with their start and end apart: 4, of which 3 were waited for; matrix products, arithmetic and copies ran while one was open for 31% of the time, Pallas kernels for 0%

commit v1 on v0

--- a/solution.py
+++ b/solution.py
@@ -131,7 +131,10 @@
         )
     mixed = mixed.astype(jnp.bfloat16)
     spread = mixed.reshape(windows, QUARTERS, quarter_tokens, width)
-    gathered = lax.all_to_all(spread, "mp", split_axis=1, concat_axis=1, tiled=True)
+    gathered = jnp.concatenate(
+        lax.all_to_all(jnp.stack(jnp.split(spread, lax.axis_size("mp"), axis=1)), "mp", 0, 0),
+        axis=1,
+    )
     out_grouped = out_full_t.reshape(model_width, QUARTERS, width)
     branch = lax.dot_general(
         gathered, out_grouped, (((1, 3), (1, 2)), ((), ())), preferred_element_type=jnp.float32

time: 357 us -> 357 us (level)
  no operation moved by 1% of the time
where the time goes in v1:
time: 357 us; the launch traced here: 356 us
  waiting for transfers between devices  173 us (48%)
  matrix products  66.5 us (19%)
  local copies, waits for them, and re-layouts  51.6 us (14%)
  other arithmetic  33.9 us (9%)
  between operations  18.9 us (5%)
  starting transfers between devices  11.8 us (3%)
    all_gather x1, waiting for transfers between devices, local(): joined = lax.all_gather(fused_rows, 'seq', axis=0, tiled=True)  71.3 us
    all_to_all x1, waiting for transfers between devices, local(): lax.all_to_all(sectioned, ('seq', 'mp'), split_axis=0, concat_axis=0, til...  67.9 us
    all_to_all x1, waiting for transfers between devices, local(): lax.all_to_all(jnp.stack(jnp.split(spread, lax.axis_size('mp'), axis=1)),...  33.7 us
    dot_general x4, matrix products, local(): jnp.einsum('wqk,wkd->wqd', weights, own_values, preferred_element_type=jn...  26 us
    dot_general x1, matrix products, local(): projected = jnp.dot(normed, fused, preferred_element_type=jnp.float32)  23.8 us
    convert_element_type x1, other arithmetic, local(): turned.astype(jnp.bfloat16).reshape(windows, window_tokens, 2 * width)  10.4 us
    dot_general x4, matrix products, local(): jnp.einsum('wqd,wkd->wqk', picked, key_block, preferred_element_type=jnp....  9.44 us
    reshape x2, local copies, waits for them, and re-layouts, local(): block_out.reshape(page_count, quarter_tokens, QUARTERS, share_width)  8.5 us
  transfers between devices with their start and end apart: 4, of which 3 were waited for; matrix products, arithmetic and copies ran while one was open for 31% of the time, Pallas kernels for 0%

profile of v1, /device:TPU:1, one launch (start us, length us, event | category | flops | bytes accessed | tf_op | source)
XLA Modules:
  0.0 355.6 jit_solution(4224788765711841023)
XLA Ops:
  8.7 1.5 concatenate.24
  12.5 6.1 %fusion.4 = f32[4096]{0:T(1024)S(1)} fusion(bf16[4096,1280]{1,0:T(8,128)(2,1)} %param.6), kind=kLoop, calls=%fused_computation.7 | loop fusion | flops 15724544 | bytes 10502144 | tf_op jit(solution)/shard_map/reduce_sum | solution.py:60
  18.7 4.8 %fusion.69 = (f32[4096,80]{0,1:T(8,128)S(1)}, f32[4096,80]{0,1:T(8,128)S(1)}) fusion(f32[4096,20]{0,1:T(8,128)S(1)} %get-tuple-element.23, f32[4096,20]{0,1:T(8,128)S(1)} %get-tuple-element.22), kind=kLoop, calls=%fused_computation.89 | loop fusion | flops 983040 | bytes 3276800 | tf_op jit(solution)/shard_map/cos | solution.py:23
  23.5 71.3 %all-gather.6.cloned.1.call-done = bf16[64,20,1920]{2,1,0:T(8,128)(2,1)} async-done(((bf16[1,20,1920]{2,1,0:T(8,128)(2,1)}), bf16[64,20,1920]{2,1,0:T(8,128)(2,1)}) %all-gather.6.cloned.1.call-update) | async-done | bytes 4915216 | tf_op jit(solution)/shard_map/all_gather | solution.py:96
  94.8 7.5 %reshape.670 = bf16[1280,1920]{1,0:T(8,128)(2,1)} reshape(bf16[64,20,1920]{2,1,0:T(8,128)(2,1)} %all-gather.6.cloned.1.call-done) | data formatting | bytes 9830400
  102.3 2.6 slice.72
  104.9 2.2 copy.82
  107.2 23.8 %fusion.6 = f32[4096,1600]{0,1:T(8,128)} fusion(bf16[4096,1280]{1,0:T(8,128)(2,1)} %param.6, f32[4096]{0:T(1024)S(1)} %add_rsqrt_fusion, bf16[1280,1920]{1,0:T(8,128)(2,1)} %reshape.670), kind=kOutput, calls=%fused_computation.9 | convolution fusion | flops 16792944640 | bytes 40976384 | tf_op jit(solution)/shard_map/dot_general | solution.py:108
  131.0 4.4 %slice.125 = bf16[4096,320]{0,1:T(8,128)(2,1)} slice(f32[4096,1600]{0,1:T(8,128)} %fusion.6), slice={[0:4096], [1280:1600]} | slice | bytes 5242880 | tf_op jit(solution)/shard_map/slice | solution.py:114
  135.4 10.4 %fusion.9 = bf16[4096,640]{0,1:T(8,128)(2,1)} fusion(f32[4096,1600]{0,1:T(8,128)} %fusion.6, f32[4096,80]{0,1:T(8,128)S(1)} %get-tuple-element.15, f32[4096,80]{0,1:T(8,128)S(1)} %get-tuple-element.14), kind=kLoop, calls=%fused_computation.12 | loop fusion | flops 10485760 | bytes 28835840 | tf_op jit(solution)/shard_map/convert_element_type | solution.py:111
  145.8 7.9 %copy.72 = bf16[4096,640]{1,0:T(8,128)(2,1)} copy(bf16[4096,640]{0,1:T(8,128)(2,1)} %fusion.9) | data formatting | bytes 10485760 | tf_op jit(solution)/shard_map/convert_element_type | solution.py:111
  153.7 3.5 copy.73
  157.2 5.4 %fusion.20 = f32[64,64,64]{1,2,0:T(8,128)S(1)} fusion(pred[320]{0:T(512)(128)(4,1)S(1)} %broadcast_compare_fusion.1, bf16[64,64,640]{2,1,0:T(8,128)(2,1)} %bitcast.74), kind=kOutput, calls=%fused_computation.29 | convolution fusion | flops 169082880 | bytes 7340352 | tf_op jit(solution)/shard_map/wqd,wkd->wqk/dot_general | solution.py:122
  163.3 1.4 fusion.16
  165.3 1.4 fusion.28
  166.7 1.4 fusion.24
  169.4 5.4 %fusion.22 = f32[64,64,320]{2,1,0:T(8,128)} fusion(bf16[64,64,320]{2,1,0:T(8,128)(2,1)S(1)} %bitcast.70, pred[320]{0:T(512)(128)(4,1)S(1)} %broadcast_compare_fusion.3, f32[64,64]{1,0:T(8,128)S(1)} %fusion.127, f32[64,64,64]{1,2,0:T(8,128)} %copy-done.7), kind=kOutput, calls=%fused_computation.31 | convolution fusion | flops 170135616 | bytes 8929600 | tf_op jit(solution)/shard_map/wqk,wkd->wqd/dot_general | solution.py:129
  174.8 5.4 %fusion.14 = f32[64,64,320]{2,1,0:T(8,128)} fusion(bf16[64,64,320]{2,1,0:T(8,128)(2,1)S(1)} %bitcast.71, pred[320]{0:T(512)(128)(4,1)S(1)} %broadcast_compare_fusion, f32[64,64]{1,0:T(8,128)S(1)} %fusion.125, f32[64,64,64]{1,2,0:T(8,128)} %copy-done.6), kind=kOutput, calls=%fused_computation.23 | convolution fusion | flops 170135616 | bytes 8929600 | tf_op jit(solution)/shard_map/wqk,wkd->wqd/dot_general | solution.py:129
  180.2 5.3 %fusion.18 = f32[64,64,320]{2,1,0:T(8,128)} fusion(bf16[64,64,320]{2,1,0:T(8,128)(2,1)S(1)} %bitcast.72, pred[320]{0:T(512)(128)(4,1)S(1)} %broadcast_compare_fusion.1, f32[64,64]{1,0:T(8,128)S(1)} %fusion.126, f32[64,64,64]{1,2,0:T(8,128)} %copy-done.5), kind=kOutput, calls=%fused_computation.27 | convolution fusion | flops 170135616 | bytes 8929600 | tf_op jit(solution)/shard_map/wqk,wkd->wqd/dot_general | solution.py:129
  185.5 9.9 %add_convert_fusion = bf16[64,64,320]{2,1,0:T(8,128)(2,1)S(1)} fusion(f32[64,64,320]{2,1,0:T(8,128)} %fusion.14, f32[64,64,320]{2,1,0:T(8,128)} %fusion.18, f32[64,64,320]{2,1,0:T(8,128)} %fusion.22, bf16[64,64,320]{2,1,0:T(8,128)(2,1)} %bitcast.73, pred[320]{0:T(512)(128)(4,1)S(1)} %broadcast_compare_fusion.2, f32[64,64]{1,0:T(8,128)S(1)} %fusion.128, ...), kind=kOutput, calls=%fused_computation.15 | convolution fusion | flops 175378496 | bytes 22036800 | tf_op jit(solution)/shard_map/wqk,wkd->wqd/dot_general | solution.py:129
  195.7 2.1 pad_maximum_fusion
  197.8 3.9 %all-to-all-start = ((bf16[4,64,1,16,320]{4,3,1,2,0:T(8,128)(2,1)}), bf16[4,64,1,16,320]{4,3,1,2,0:T(8,128)(2,1)S(1)}, u32[]{:S(2)}, u32[]{:S(2)}) async-start(bf16[4,64,1,16,320]{4,3,1,2,0:T(8,128)(2,1)} %pad_maximum_fusion), calls=%async_computation | async-start | bytes 6291456 | tf_op jit(solution)/shard_map/all_to_all | solution.py:135
  201.7 3.4 constant_dynamic-slice_fusion
  205.1 33.7 %all-to-all-done = bf16[4,64,1,16,320]{4,3,1,2,0:T(8,128)(2,1)S(1)} async-done(((bf16[4,64,1,16,320]{4,3,1,2,0:T(8,128)(2,1)}), bf16[4,64,1,16,320]{4,3,1,2,0:T(8,128)(2,1)S(1)}, u32[]{:S(2)}, u32[]{:S(2)}) %all-to-all-start) | async-done | bytes 2621472 | tf_op jit(solution)/shard_map/all_to_all | solution.py:135
  238.7 7.3 %fusion.11 = bf16[1024,1280]{1,0:T(8,128)(2,1)} fusion(bf16[1024,1280]{1,0:T(8,128)(2,1)} %bitcast.79, bf16[1024,4,320]{2,0,1:T(8,128)(2,1)S(1)} %bitcast.78, bf16[1280,4,320]{0,2,1:T(8,128)(2,1)} %bitcast.83), kind=kOutput, calls=%fused_computation.18 | convolution fusion | flops 3359375360 | bytes 11141120 | tf_op jit(solution)/shard_map/dot_general | solution.py:139
  246.0 6.1 %reshape.656 = bf16[64,16,4,320]{3,2,1,0:T(4,128)(2,1)S(1)} reshape(bf16[1024,1280]{1,0:T(8,128)(2,1)} %fusion.11) | data formatting | bytes 5242880 | tf_op jit(solution)/shard_map/reshape | solution.py:148
  252.1 2.4 copy.84
  254.5 7.8 %all-to-all-start.1 = ((bf16[256,16,320]{2,1,0:T(8,128)(2,1)}), bf16[256,16,320]{2,1,0:T(8,128)(2,1)S(1)}, u32[]{:S(2)}, u32[]{:S(2)}) async-start(bf16[256,16,320]{2,1,0:T(8,128)(2,1)} %bitcast.68), calls=%async_computation.1 | async-start | bytes 6291456 | tf_op jit(solution)/shard_map/all_to_all | solution.py:152
  270.4 67.9 %all-to-all-done.1 = bf16[256,16,320]{2,1,0:T(8,128)(2,1)S(1)} async-done(((bf16[256,16,320]{2,1,0:T(8,128)(2,1)}), bf16[256,16,320]{2,1,0:T(8,128)(2,1)S(1)}, u32[]{:S(2)}, u32[]{:S(2)}) %all-to-all-start.1) | async-done | bytes 2621472 | tf_op jit(solution)/shard_map/all_to_all | solution.py:152
  338.3 2.7 gather_fusion
  341.0 5.0 %fusion.13 = bf16[4096,320]{1,0:T(8,128)(2,1)S(1)} fusion(bf16[256,16,320]{2,1,0:T(8,128)(2,1)} %gather_fusion, pred[4096]{0:T(1024)(128)(4,1)S(1)} %broadcast_in_dim.141, pred[4096]{0:T(1024)(128)(4,1)S(1)} %broadcast_in_dim.135), kind=kLoop, calls=%fused_computation.22 | loop fusion | flops 2621440 | bytes 5251072 | tf_op jit(solution)/shard_map/vmap(jit(_where))/select_n | solution.py:164
  346.0 2.7 copy.85
  (67 shorter events, 10.3 us)
Async XLA Ops:
  6.5 88.3 %all-gather.6.cloned.1.call-start = ((), (), s32[]{:S(2)}) async-start(), calls=%async_computation.3 | async-start | bytes 5990400 | tf_op jit(solution)/shard_map/all_gather | solution.py:96
  10.2 228.5 %all-gather.4.cloned.1.call-start = ((), (), s32[]{:S(2)}) async-start(), calls=%async_computation.2 | async-start | bytes 4096000 | tf_op jit(solution)/shard_map/all_gather | solution.py:99
  157.2 22.9 %copy-start = (bf16[4096,320]{1,0:T(8,128)(2,1)}, bf16[4096,320]{1,0:T(8,128)(2,1)S(1)}, u32[]{:S(2)}) copy-start(bf16[4096,320]{1,0:T(8,128)(2,1)S(1)} %copy.73) | copy-start | bytes 7864324
  157.2 6.0 %copy-start.1 = (bf16[4096,640]{1,0:T(8,128)(2,1)S(1)}, bf16[4096,640]{1,0:T(8,128)(2,1)}, u32[]{:S(2)}) copy-start(bf16[4096,640]{1,0:T(8,128)(2,1)} %copy.72) | copy-start | bytes 15728644
  162.6 2.0 copy-start.5
  164.7 2.0 copy-start.6
  166.7 2.0 copy-start.2
  168.1 1.3 copy-start.7
  197.8 41.0 %all-to-all-start = ((bf16[4,64,1,16,320]{4,3,1,2,0:T(8,128)(2,1)}), bf16[4,64,1,16,320]{4,3,1,2,0:T(8,128)(2,1)S(1)}, u32[]{:S(2)}, u32[]{:S(2)}) async-start(bf16[4,64,1,16,320]{4,3,1,2,0:T(8,128)(2,1)} %pad_maximum_fusion), calls=%async_computation | async-start | bytes 6291456 | tf_op jit(solution)/shard_map/all_to_all | solution.py:135
  254.5 7.8 %copy-start.3 = (s32[64]{0:T(128)S(1)}, s32[64]{0:T(128)}, u32[]{:S(2)}) copy-start(s32[64]{0:T(128)} %param.10) | copy-start | bytes 772
  254.5 11.0 %copy-start.4 = (s32[64]{0:T(128)S(1)}, s32[64]{0:T(128)}, u32[]{:S(2)}) copy-start(s32[64]{0:T(128)} %param.9) | copy-start | bytes 772
  254.5 83.8 %all-to-all-start.1 = ((bf16[256,16,320]{2,1,0:T(8,128)(2,1)}), bf16[256,16,320]{2,1,0:T(8,128)(2,1)S(1)}, u32[]{:S(2)}, u32[]{:S(2)}) async-start(bf16[256,16,320]{2,1,0:T(8,128)(2,1)} %bitcast.68), calls=%async_computation.1 | async-start | bytes 6291456 | tf_op jit(solution)/shard_map/all_to_all | solution.py:152
Sparse Core Ops, SparseCore 0:
  10.4 84.3 all-gather.5
  107.3 39.4 all-gather.3
